TPU v7x, 256 devices: a whole 4x4x8 slice. The times are simulated.
256 devices in a mesh: section: 2 (over core), tok: 32 (over z, y), rep: 4 (over x).
Axes of the slice: x: 4, y: 4, z: 8, core: 2. Of those that a mesh axis runs over, the one named last changes fastest.
Arguments:
- inputs: bfloat16 [2, 4096, 1024], P(None, 'tok')
- segment_ids: int32 [2, 4096], replicated, may hold values from 0 to 7, as said below
- picks: int32 [2, 4096, 2], P(None, 'tok'), may hold values from 0 to 15, all different within a row; in each aligned block of 128 rows (0 to 127, 128 to 255, ..., all dimensions but the last counted through in order) at most 20 rows name the same one
- page_table: int32 [2, 32], replicated, may hold values from 0 to 31, each once within a row
- norm_gains: float32 [2, 2, 1024], P('section'), may hold values from 0.1 to 1.9
- attn_qkv: bfloat16 [2, 1024, 3, 1024], P('section', None, None, 'rep')
- attn_out: bfloat16 [2, 1024, 1024], P('section', 'rep'), may hold values from -0.1875 to 0.1875
- router: bfloat16 [2, 1024, 16], P('section')
- expert_in: bfloat16 [2, 32, 1024, 2, 1408], P('section', 'tok', None, None, 'rep'), may hold values from -0.1875 to 0.1875
- expert_out: bfloat16 [2, 32, 1408, 1024], P('section', 'tok', 'rep')
Outputs:
- layer_out: bfloat16 [2, 2, 4096, 1024], P('section', None, 'tok')
- kv_pages: bfloat16 [2, 2, 32, 128, 2, 1024], P('section', None, 'tok', None, None, 'rep')
Inputs may be any that keep to these rules, and one draw needn't show every extreme that they name: `picks`: within the tokens of one index of tok in one micro-batch, at most 20 tokens pick one expert, and some expert is picked by exactly 20. `segment_ids`: ids never fall along a micro-batch; every prompt has at least one token, a prompt spans at most 2048 tokens and one spans exactly 2048. `page_table`: each row is a permutation.
All inputs are finite; a program needn't handle non-finite values.
Results may differ from a plain program's by a relative error of at most 0.034.
Values may be sent and summed in bfloat16 or wider, within the bound.
No kernel may reach another device: no remote copies, remote signals or barrier semaphores. Data moves between devices by JAX's collectives and lax.ppermute only.
A program may use at most 128 MiB of HBM per device.

v0:
```python
import jax
import jax.numpy as jnp
from jax import lax
from jax.sharding import PartitionSpec as P

HEAD_DIM = 64
TOP = 2
PAGE = 128
CAP = 20
NEG_FILL = -1e30


def shifted(value, axis, steps):
    count = lax.axis_size(axis)
    first, last = (max(0, -steps), min(count, count - steps))
    return lax.ppermute(value, axis, [(source, source + steps) for source in range(first, last)])


def rms_scale(values, gains):
    return values * lax.rsqrt(jnp.mean(values * values, axis=-1, keepdims=True) + 1e-06) * gains


def attend(carry, queries, keys_vals, seg_query, pos_query, seg_key, pos_key):
    run_max, run_sum, run_acc = carry
    heads_here = run_acc.shape[0]
    head_size = run_acc.shape[2]
    rows_key = keys_vals.shape[0]
    key_part = keys_vals[:, 0].reshape(rows_key, heads_here, head_size)
    val_part = keys_vals[:, 1].reshape(rows_key, heads_here, head_size).astype(jnp.float32)
    scores = jnp.einsum(
        "thd,nhd->htn", queries, key_part, preferred_element_type=jnp.float32
    ) * head_size ** (-0.5)
    visible = (seg_query[:, None] == seg_key[None, :]) & (pos_query[:, None] >= pos_key[None, :])
    masked = jnp.where(visible[None], scores, NEG_FILL)
    new_max = jnp.maximum(run_max, jnp.max(masked, axis=-1))
    weights = jnp.where(visible[None], jnp.exp(masked - new_max[..., None]), 0.0)
    decay = jnp.exp(run_max - new_max)
    run_sum = run_sum * decay + jnp.sum(weights, axis=-1)
    run_acc = run_acc * decay[..., None] + jnp.einsum(
        "htn,nhd->htd", weights, val_part, precision=lax.Precision.HIGHEST
    )
    return (new_max, run_sum, run_acc)


def place_pages(pages, keys_vals, table_row, tok_index):
    rows_here = keys_vals.shape[0]
    blocks_dev = pages.shape[0]
    page_rows = pages.shape[1]
    block_ids = jnp.arange(table_row.shape[0], dtype=jnp.int32)
    wanted = tok_index * blocks_dev + 0
    source = jnp.sum(jnp.where(table_row == wanted, block_ids, 0))
    offset = source * page_rows
    inside = (offset >= 0) & (offset + page_rows <= rows_here)
    block = lax.dynamic_slice_in_dim(
        keys_vals, jnp.clip(offset, 0, rows_here - page_rows), page_rows, 0
    )
    updated = [jnp.where(inside, block, pages[0])]
    return jnp.stack(updated)


def per_device(
    inputs,
    segment_ids,
    picks,
    page_table,
    norm_gains,
    attn_qkv,
    attn_out,
    router,
    expert_in,
    expert_out,
):
    section_index = lax.axis_index("section")
    tok_index = lax.axis_index("tok")
    tok_count = lax.axis_size("tok")
    micro_count = inputs.shape[0]
    tok_rows = inputs.shape[1]
    width = inputs.shape[2]
    col_width = attn_qkv.shape[3]
    head_count = col_width // HEAD_DIM
    experts_all = router.shape[2]
    local_pieces = expert_in.shape[1]
    split_count = local_pieces * tok_count // experts_all
    blocks_dev = tok_rows // PAGE
    row_ids = jnp.arange(tok_rows, dtype=jnp.int32)
    pos_query = tok_index * tok_rows + row_ids
    gains = norm_gains[0]
    w_qkv = attn_qkv[0].reshape(width, 3 * col_width)
    w_out = attn_out[0]
    w_router = router[0]
    w_in = expert_in[0]
    w_down = expert_out[0]
    outputs = [jnp.zeros((tok_rows, width), jnp.bfloat16) for slot_micro in range(micro_count)]
    page_out = [
        jnp.zeros((blocks_dev, PAGE, 2, col_width), jnp.bfloat16)
        for slot_micro in range(micro_count)
    ]
    received = jnp.zeros((tok_rows, width), jnp.bfloat16)
    for round_index in range(micro_count + 1):
        own_micro = round_index - section_index
        micro_index = jnp.clip(own_micro, 0, micro_count - 1)
        fresh = inputs[min(round_index, micro_count - 1)]
        layer_in = jnp.where(section_index == 0, fresh, received)
        seg_all = lax.dynamic_index_in_dim(segment_ids, micro_index, 0, keepdims=False)
        seg_query = lax.dynamic_slice_in_dim(seg_all, tok_index * tok_rows, tok_rows)
        table_row = lax.dynamic_index_in_dim(page_table, micro_index, 0, keepdims=False)
        pick_rows = lax.dynamic_index_in_dim(picks, micro_index, 0, keepdims=False)
        resid = layer_in.astype(jnp.float32)
        normed = rms_scale(resid, gains[0]).astype(jnp.bfloat16)
        projected = jnp.dot(normed, w_qkv, preferred_element_type=jnp.float32).astype(jnp.bfloat16)
        projected = projected.reshape(tok_rows, 3, col_width)
        queries = projected[:, 0].reshape(tok_rows, head_count, HEAD_DIM)
        keys_vals = projected[:, 1:]
        soft_init = (
            jnp.full((head_count, tok_rows), NEG_FILL, jnp.float32),
            jnp.zeros((head_count, tok_rows), jnp.float32),
            jnp.zeros((head_count, tok_rows, HEAD_DIM), jnp.float32),
        )
        empty_pages = jnp.zeros((blocks_dev, PAGE, 2, col_width), jnp.bfloat16)
        piece = lax.all_gather(keys_vals, "tok", axis=0, tiled=True)
        rows_key = piece.shape[0]
        step_rows = 1024
        while rows_key % step_rows != 0:
            step_rows = step_rows // 2
        turns = rows_key // step_rows

        def key_block(index, soft_now):
            start = index * step_rows
            block = lax.dynamic_slice_in_dim(piece, start, step_rows, 0)
            seg_key = lax.dynamic_slice_in_dim(seg_all, start, step_rows)
            pos_key = start + jnp.arange(step_rows, dtype=jnp.int32)
            return attend(soft_now, queries, block, seg_query, pos_query, seg_key, pos_key)

        soft_next = lax.fori_loop(0, turns, key_block, soft_init)
        pages = place_pages(empty_pages, piece, table_row, tok_index)
        run_max, run_sum, run_acc = soft_next
        context = (
            (run_acc / run_sum[..., None])
            .transpose(1, 0, 2)
            .reshape(tok_rows, col_width)
            .astype(jnp.bfloat16)
        )
        attn_part = jnp.dot(context, w_out, preferred_element_type=jnp.float32)
        mid = resid + lax.psum(attn_part, "rep")
        normed_mid = rms_scale(mid, gains[1]).astype(jnp.bfloat16)
        logits = jnp.dot(normed_mid, w_router, preferred_element_type=jnp.float32)
        expert_ids = jnp.arange(experts_all, dtype=jnp.int32)
        chosen = (pick_rows[:, :, None] == expert_ids[None, None, :]).astype(jnp.int32)
        picked_logit = jnp.sum(chosen.astype(jnp.float32) * logits[:, None, :], axis=-1)
        top_logit = jnp.max(picked_logit, axis=-1, keepdims=True)
        raised = jnp.exp(picked_logit - top_logit)
        gate_vals = raised / jnp.sum(raised, axis=-1, keepdims=True)
        ordered = chosen.transpose(1, 0, 2).reshape(TOP * tok_rows, experts_all)
        slot_of = jnp.sum((jnp.cumsum(ordered, axis=0) - 1) * ordered, axis=-1)
        flat_slot = pick_rows.T.reshape(TOP * tok_rows) * CAP + slot_of
        slot_ids = jnp.arange(experts_all * CAP, dtype=jnp.int32)
        hits = (flat_slot[:, None] == slot_ids[None, :]).astype(jnp.int32)
        hits = jnp.sum(hits.reshape(TOP, tok_rows, experts_all * CAP), axis=0).astype(jnp.bfloat16)
        dispatch = lax.dot_general(
            hits, normed_mid, (((0,), (0,)), ((), ())), preferred_element_type=jnp.float32
        ).astype(jnp.bfloat16)
        copies = jnp.broadcast_to(
            dispatch.reshape(experts_all, 1, CAP, width), (experts_all, split_count, CAP, width)
        )
        copies = copies.reshape(tok_count, local_pieces, CAP, width)
        act = jnp.einsum(
            "secd,edgf->secgf",
            lax.all_to_all(copies, "tok", split_axis=0, concat_axis=0, tiled=True),
            w_in,
            preferred_element_type=jnp.float32,
        )
        hidden = (jax.nn.gelu(act[..., 0, :]) * act[..., 1, :]).astype(jnp.bfloat16)
        returned = lax.all_to_all(
            jnp.einsum("secf,efd->secd", hidden, w_down, preferred_element_type=jnp.float32).astype(
                jnp.bfloat16
            ),
            "tok",
            split_axis=0,
            concat_axis=0,
            tiled=True,
        )
        summed = jnp.sum(
            returned.reshape(experts_all, split_count, CAP, width).astype(jnp.float32), axis=1
        )
        summed = summed.reshape(experts_all * CAP, width)
        gathered = jnp.take(summed, flat_slot, axis=0).reshape(TOP, tok_rows, width)
        expert_local = jnp.sum(gate_vals.T[:, :, None] * gathered, axis=0)
        expert_total = lax.psum(expert_local, "rep")
        layer_result = (mid + expert_total).astype(jnp.bfloat16)
        for slot_micro in range(micro_count):
            if slot_micro == round_index or slot_micro == round_index - 1:
                taken = own_micro == slot_micro
                outputs[slot_micro] = jnp.where(taken, layer_result, outputs[slot_micro])
                page_out[slot_micro] = jnp.where(taken, pages, page_out[slot_micro])
        if round_index < micro_count:
            received = shifted(layer_result, "section", 1)
    return (jnp.stack(outputs)[None], jnp.stack(page_out)[None])


def solution(mesh):
    return jax.shard_map(
        per_device,
        mesh=mesh,
        in_specs=(
            P(None, "tok", None),
            P(),
            P(None, "tok", None),
            P(),
            P("section", None, None),
            P("section", None, None, "rep"),
            P("section", "rep", None),
            P("section", None, None),
            P("section", "tok", None, None, "rep"),
            P("section", "tok", "rep", None),
        ),
        out_specs=(P("section", None, "tok", None), P("section", None, "tok", None, None, "rep")),
        check_vma=False,
    )
```

profile of v0, /device:TPU:8, one launch (start us, length us, event | category | flops | bytes accessed | tf_op | source)
XLA Modules:
  0.0 1003.8 jit_solution(15672951469307340651)
XLA Ops:
  9.3 1.7 copy.83
  18.9 1.5 constant_dynamic-slice_fusion.12
  20.4 79.9 %all-gather.4.cloned.1.call-done = bf16[4096,2,256]{0,2,1:T(8,128)(2,1)} async-done(((bf16[128,2,256]{0,2,1:T(8,128)(2,1)}), bf16[4096,2,256]{0,2,1:T(8,128)(2,1)}) %all-gather.4.cloned.1.call-update) | async-done | bytes 4194320 | tf_op jit(solution)/shard_map/all_gather | solution.py:120
  100.3 34.9 %while.54 = (s32[]{:T(128)}, f32[4,128]{1,0:T(4,128)S(1)}, f32[4,128]{1,0:T(4,128)S(1)}, f32[4,128,64]{1,2,0:T(8,128)}, s32[128]{0:T(128)}, /*index=5*/s32[4096]...) while((s32[]{:T(128)}, f32[4,128]{1,0:T(4,128)S(1)}, ...), condition=%wide.region_4.5_spmd.clone, body=%wide.region_1.4_spmd.clone.sunk | while | flops 476548736 | bytes 14800775 | solution.py:134
  101.0 1.7 compare_and_fusion.9
  102.7 2.1 constant_dynamic-slice_fusion.18
  109.7 1.7 compare_and_fusion.9
  111.4 2.1 constant_dynamic-slice_fusion.18
  118.5 1.7 compare_and_fusion.9
  120.1 2.1 constant_dynamic-slice_fusion.18
  122.9 1.5 fusion.224
  127.2 1.7 compare_and_fusion.9
  128.9 2.1 constant_dynamic-slice_fusion.18
  136.2 2.1 fusion.102
  140.8 46.1 %all-reduce.7.cloned.1.call-done = f32[128,1024]{1,0:T(8,128)} async-done(((f32[128,1024]{1,0:T(8,128)}), f32[128,1024]{1,0:T(8,128)}) %all-reduce.7.cloned.1.call-update) | async-done | bytes 524304 | tf_op jit(solution)/shard_map/psum | solution.py:144
  190.6 47.1 %all_to_all.30 = bf16[32,1,20,1024]{3,2,1,0:T(8,128)(2,1)S(1)} all-to-all(bf16[32,1,20,1024]{3,2,1,0:T(8,128)(2,1)S(1)} %bitcast.386), channel_id=1, replica_groups=mesh['section'=2,'tok'=32,'rep'=4] {'tok'}, dimensions={0} | all-to-all | bytes 2621440 | tf_op jit(solution)/shard_map/all_to_all | solution.py:168
  237.7 1.8 convolution_bitcast_fusion.2
  240.4 1.9 copy.87
  242.3 5.7 all-to-all-start.1
  251.2 33.0 %all-to-all-done.1 = bf16[32,1,20,1024]{3,2,1,0:T(8,128)(2,1)S(1)} async-done(((bf16[32,1,20,1024]{3,2,1,0:T(8,128)(2,1)}), bf16[32,1,20,1024]{3,2,1,0:T(8,128)(2,1)S(1)}, u32[]{:S(2)}, u32[]{:S(2)}) %all-to-all-start.1) | async-done | bytes 1310752 | tf_op jit(solution)/shard_map/all_to_all | solution.py:173
  284.2 1.5 convert_reduce_fusion.2
  287.2 2.2 gather_fusion
  291.7 45.9 %all-reduce.9.cloned.1.call-done = f32[128,1024]{1,0:T(8,128)} async-done(((f32[128,1024]{1,0:T(8,128)}), f32[128,1024]{1,0:T(8,128)}) %all-reduce.9.cloned.1.call-update) | async-done | bytes 524304 | tf_op jit(solution)/shard_map/psum | solution.py:188
  348.5 79.2 %all-gather.6.cloned.1.call-done = bf16[4096,2,256]{0,2,1:T(8,128)(2,1)} async-done(((bf16[128,2,256]{0,2,1:T(8,128)(2,1)}), bf16[4096,2,256]{0,2,1:T(8,128)(2,1)}) %all-gather.6.cloned.1.call-update) | async-done | bytes 4194320 | tf_op jit(solution)/shard_map/all_gather | solution.py:120
  427.7 35.0 %while.55 = (s32[]{:T(128)}, f32[4,128]{1,0:T(4,128)S(1)}, f32[4,128]{1,0:T(4,128)S(1)}, f32[4,128,64]{1,2,0:T(8,128)}, s32[128]{0:T(128)}, /*index=5*/s32[4096]...) while((s32[]{:T(128)}, f32[4,128]{1,0:T(4,128)S(1)}, ...), condition=%wide.region_21.23_spmd.clone, body=%wide.region_18.22_spmd.clone.sunk | while | flops 476548736 | bytes 14800775 | solution.py:134
  428.4 1.7 compare_and_fusion.10
  430.1 2.1 constant_dynamic-slice_fusion.19
  432.8 1.5 fusion.231
  437.1 1.7 compare_and_fusion.10
  438.8 2.1 constant_dynamic-slice_fusion.19
  445.9 1.7 compare_and_fusion.10
  447.5 2.1 constant_dynamic-slice_fusion.19
  454.6 1.7 compare_and_fusion.10
  456.3 2.1 constant_dynamic-slice_fusion.19
  463.6 2.1 fusion.100
  468.8 45.5 %all-reduce.11.cloned.1.call-done = f32[128,1024]{1,0:T(8,128)} async-done(((f32[128,1024]{1,0:T(8,128)}), f32[128,1024]{1,0:T(8,128)}) %all-reduce.11.cloned.1.call-update) | async-done | bytes 524304 | tf_op jit(solution)/shard_map/psum | solution.py:144
  517.3 47.1 %all_to_all.31 = bf16[32,1,20,1024]{3,2,1,0:T(8,128)(2,1)S(1)} all-to-all(bf16[32,1,20,1024]{3,2,1,0:T(8,128)(2,1)S(1)} %bitcast.387), channel_id=1, replica_groups=mesh['section'=2,'tok'=32,'rep'=4] {'tok'}, dimensions={0} | all-to-all | bytes 2621440 | tf_op jit(solution)/shard_map/all_to_all | solution.py:168
  564.4 1.8 convolution_bitcast_fusion.1
  567.1 1.9 copy.93
  569.0 5.7 all-to-all-start.3
  577.6 33.2 %all-to-all-done.3 = bf16[32,1,20,1024]{3,2,1,0:T(8,128)(2,1)S(1)} async-done(((bf16[32,1,20,1024]{3,2,1,0:T(8,128)(2,1)}), bf16[32,1,20,1024]{3,2,1,0:T(8,128)(2,1)S(1)}, u32[]{:S(2)}, u32[]{:S(2)}) %all-to-all-start.3) | async-done | bytes 1310752 | tf_op jit(solution)/shard_map/all_to_all | solution.py:173
  613.8 2.2 gather_fusion.1
  618.5 46.1 %all-reduce.13.cloned.1.call-done = f32[128,1024]{1,0:T(8,128)} async-done(((f32[128,1024]{1,0:T(8,128)}), f32[128,1024]{1,0:T(8,128)}) %all-reduce.13.cloned.1.call-update) | async-done | bytes 524304 | tf_op jit(solution)/shard_map/psum | solution.py:188
  664.5 2.1 select_bitcast_fusion
  672.4 82.9 %all-gather.8.cloned.1.call-done = bf16[4096,2,256]{0,2,1:T(8,128)(2,1)} async-done(((bf16[128,2,256]{0,2,1:T(8,128)(2,1)}), bf16[4096,2,256]{0,2,1:T(8,128)(2,1)}) %all-gather.8.cloned.1.call-update) | async-done | bytes 4194320 | tf_op jit(solution)/shard_map/all_gather | solution.py:120
  755.3 34.7 %while.56 = (s32[]{:T(128)}, f32[4,128]{1,0:T(4,128)S(1)}, f32[4,128]{1,0:T(4,128)S(1)}, f32[4,128,64]{1,2,0:T(8,128)}, s32[128]{0:T(128)}, /*index=5*/s32[4096]...) while((s32[]{:T(128)}, f32[4,128]{1,0:T(4,128)S(1)}, ...), condition=%wide.region_38.40_spmd.clone, body=%wide.region_35.39_spmd.clone.sunk | while | flops 476548736 | bytes 14800775 | solution.py:134
  756.0 1.6 compare_and_fusion.11
  757.6 2.1 constant_dynamic-slice_fusion.20
  764.7 1.6 compare_and_fusion.11
  766.3 2.1 constant_dynamic-slice_fusion.20
  773.4 1.6 compare_and_fusion.11
  775.0 2.1 constant_dynamic-slice_fusion.20
  782.0 1.6 compare_and_fusion.11
  783.7 2.1 constant_dynamic-slice_fusion.20
  791.0 2.1 fusion.98
  793.9 47.8 %all-reduce.15.cloned.1.call-done = f32[128,1024]{1,0:T(8,128)} async-done(((f32[128,1024]{1,0:T(8,128)}), f32[128,1024]{1,0:T(8,128)}) %all-reduce.15.cloned.1.call-update) | async-done | bytes 524304 | tf_op jit(solution)/shard_map/psum | solution.py:144
  846.6 47.1 %all_to_all.32 = bf16[32,1,20,1024]{3,2,1,0:T(8,128)(2,1)S(1)} all-to-all(bf16[32,1,20,1024]{3,2,1,0:T(8,128)(2,1)S(1)} %bitcast.388), channel_id=1, replica_groups=mesh['section'=2,'tok'=32,'rep'=4] {'tok'}, dimensions={0} | all-to-all | bytes 2621440 | tf_op jit(solution)/shard_map/all_to_all | solution.py:168
  893.7 1.8 convolution_bitcast_fusion
  896.4 1.9 copy.99
  898.3 5.9 all-to-all-start.5
  904.6 35.8 %all-to-all-done.5 = bf16[32,1,20,1024]{3,2,1,0:T(8,128)(2,1)} async-done(((bf16[32,1,20,1024]{3,2,1,0:T(8,128)(2,1)}), bf16[32,1,20,1024]{3,2,1,0:T(8,128)(2,1)}, u32[]{:S(2)}, u32[]{:S(2)}) %all-to-all-start.5) | async-done | bytes 1310752 | tf_op jit(solution)/shard_map/all_to_all | solution.py:173
  940.3 3.1 convert_reduce_fusion
  944.8 2.1 gather_fusion.2
  954.1 41.2 %all-reduce.17.cloned.1.call-done = f32[128,1024]{1,0:T(8,128)} async-done(((f32[128,1024]{1,0:T(8,128)}), f32[128,1024]{1,0:T(8,128)}) %all-reduce.17.cloned.1.call-update) | async-done | bytes 524304 | tf_op jit(solution)/shard_map/psum | solution.py:188
  (457 shorter events, 130.0 us)
Async XLA Ops:
  7.2 230.5 %copy-start = (bf16[1,1,1024,2,352]{2,4,3,1,0:T(8,128)(2,1)S(1)}, bf16[1,1,1024,2,352]{2,4,3,1,0:T(8,128)(2,1)}, u32[]{:S(2)}) copy-start(bf16[1,1,1024,2,352]{2,4,3,1,0:T(8,128)(2,1)} %param.26) | copy-start | bytes 4325380
  7.2 3.9 copy-start.17
  7.2 93.1 %all-gather.4.cloned.1.call-start = ((), (), s32[]{:S(2)}) async-start(), calls=%async_computation.6 | async-start | bytes 4325376 | tf_op jit(solution)/shard_map/all_gather | solution.py:120
  9.3 3.1 copy-start.38
  11.0 89.3 %copy-start.7 = (bf16[1,1024,3,256]{1,3,2,0:T(8,128)(2,1)}, bf16[1,1024,3,256]{1,3,2,0:T(8,128)(2,1)S(1)}, u32[]{:S(2)}) copy-start(bf16[1,1024,3,256]{1,3,2,0:T(8,128)(2,1)S(1)} %copy.83) | copy-start | bytes 4718596
  14.2 172.7 %all-reduce.7.cloned.1.call-start = ((), (), s32[]{:S(2)}) async-start(), calls=%async_computation.7 | async-start | bytes 1048576 | tf_op jit(solution)/shard_map/psum | solution.py:144
  16.2 84.1 %copy-start.45 = (s32[2,128]{1,0:T(2,128)}, s32[2,128]{1,0:T(2,128)S(1)}, u32[]{:S(2)}) copy-start(s32[2,128]{1,0:T(2,128)S(1)} %get-tuple-element.708) | copy-start | bytes 3076
  102.7 2.1 copy-start.1
  102.7 2.1 copy-start.21
  111.4 2.1 copy-start.1
  111.4 2.1 copy-start.21
  120.1 2.1 copy-start.1
  120.1 2.1 copy-start.21
  128.8 2.1 copy-start.1
  128.8 2.1 copy-start.21
  135.2 51.6 %copy-start.18 = (bf16[2,128,1024]{2,1,0:T(8,128)(2,1)S(1)}, bf16[2,128,1024]{2,1,0:T(8,128)(2,1)}, u32[]{:S(2)}) copy-start(bf16[2,128,1024]{2,1,0:T(8,128)(2,1)} %param.18) | copy-start | bytes 1572868
  242.3 5.8 copy-start.44
  242.3 41.9 %all-to-all-start.1 = ((bf16[32,1,20,1024]{3,2,1,0:T(8,128)(2,1)}), bf16[32,1,20,1024]{3,2,1,0:T(8,128)(2,1)S(1)}, u32[]{:S(2)}, u32[]{:S(2)}) async-start(bf16[32,1,20,1024]{3,2,1,0:T(8,128)(2,1)} %copy.87), calls=%async_computation.1 | async-start | bytes 3145728 | tf_op jit(solution)/shard_map/all_to_all | solution.py:173
  248.0 89.7 %all-reduce.9.cloned.1.call-start = ((), (), s32[]{:S(2)}) async-start(), calls=%async_computation.8 | async-start | bytes 1048576 | tf_op jit(solution)/shard_map/psum | solution.py:188
  287.2 2.2 copy-start.48
  290.7 51.6 %copy-start.8 = (bf16[1,1024,3,256]{1,3,2,0:T(8,128)(2,1)S(1)}, bf16[1,1024,3,256]{1,3,2,0:T(8,128)(2,1)}, u32[]{:S(2)}) copy-start(bf16[1,1024,3,256]{1,3,2,0:T(8,128)(2,1)} %copy-done.7) | copy-start | bytes 4718596
  290.7 51.6 %copy-start.39 = (f32[1,1,1024]{2,1,0:T(1,128)S(1)}, f32[1,1,1024]{2,1,0:T(1,128)}, u32[]{:S(2)}) copy-start(f32[1,1,1024]{2,1,0:T(1,128)} %copy-done.38) | copy-start | bytes 12292
  291.7 136.0 %all-gather.6.cloned.1.call-start = ((), (), s32[]{:S(2)}) async-start(), calls=%async_computation.9 | async-start | bytes 4325376 | tf_op jit(solution)/shard_map/all_gather | solution.py:120
  339.0 2.6 copy-start.28
  339.0 2.4 collective-permute-start
  343.9 170.4 %all-reduce.11.cloned.1.call-start = ((), (), s32[]{:S(2)}) async-start(), calls=%async_computation.10 | async-start | bytes 1048576 | tf_op jit(solution)/shard_map/psum | solution.py:144
  345.2 82.5 %copy-start.31 = (s32[16,2,128]{2,0,1:T(8,128)}, s32[16,2,128]{2,0,1:T(8,128)S(1)}, u32[]{:S(2)}) copy-start(s32[16,2,128]{2,0,1:T(8,128)S(1)} %reduce-window.24) | copy-start | bytes 49156
  430.0 2.1 copy-start.3
  430.1 2.1 copy-start.23
  438.8 2.1 copy-start.3
  438.8 2.1 copy-start.23
  447.5 2.1 copy-start.3
  447.5 2.1 copy-start.23
  456.3 2.1 copy-start.3
  456.3 2.1 copy-start.23
  462.7 51.6 %copy-start.16 = (bf16[128,1024]{1,0:T(8,128)(2,1)S(1)}, bf16[128,1024]{1,0:T(8,128)(2,1)}, u32[]{:S(2)}) copy-start(bf16[128,1024]{1,0:T(8,128)(2,1)} %copy-done.15) | copy-start | bytes 786436
  569.0 5.8 copy-start.42
  569.0 41.9 %all-to-all-start.3 = ((bf16[32,1,20,1024]{3,2,1,0:T(8,128)(2,1)}), bf16[32,1,20,1024]{3,2,1,0:T(8,128)(2,1)S(1)}, u32[]{:S(2)}, u32[]{:S(2)}) async-start(bf16[32,1,20,1024]{3,2,1,0:T(8,128)(2,1)} %copy.93), calls=%async_computation.3 | async-start | bytes 3145728 | tf_op jit(solution)/shard_map/all_to_all | solution.py:173
  574.7 89.8 %all-reduce.13.cloned.1.call-start = ((), (), s32[]{:S(2)}) async-start(), calls=%async_computation.11 | async-start | bytes 1048576 | tf_op jit(solution)/shard_map/psum | solution.py:188
  613.8 2.2 copy-start.49
  616.0 48.5 %copy-start.29 = (bf16[128,1024]{1,0:T(8,128)(2,1)S(1)}, bf16[128,1024]{1,0:T(8,128)(2,1)}, u32[]{:S(2)}) copy-start(bf16[128,1024]{1,0:T(8,128)(2,1)} %copy-done.28) | copy-start | bytes 786436
  618.4 51.6 %copy-start.9 = (bf16[1,1024,3,256]{1,3,2,0:T(8,128)(2,1)S(1)}, bf16[1,1024,3,256]{1,3,2,0:T(8,128)(2,1)}, u32[]{:S(2)}) copy-start(bf16[1,1024,3,256]{1,3,2,0:T(8,128)(2,1)} %copy-done.7) | copy-start | bytes 4718596
  618.4 51.6 %copy-start.40 = (f32[1,1,1024]{2,1,0:T(1,128)S(1)}, f32[1,1,1024]{2,1,0:T(1,128)}, u32[]{:S(2)}) copy-start(f32[1,1,1024]{2,1,0:T(1,128)} %copy-done.38) | copy-start | bytes 12292
  618.4 136.9 %all-gather.8.cloned.1.call-start = ((), (), s32[]{:S(2)}) async-start(), calls=%async_computation.12 | async-start | bytes 4325376 | tf_op jit(solution)/shard_map/all_gather | solution.py:120
  664.5 4.6 copy-start.19
  666.6 2.6 copy-start.25
  666.6 2.4 collective-permute-start.1
  671.5 170.2 %all-reduce.15.cloned.1.call-start = ((), (), s32[]{:S(2)}) async-start(), calls=%async_computation.13 | async-start | bytes 1048576 | tf_op jit(solution)/shard_map/psum | solution.py:144
  757.6 2.1 copy-start.5
  757.6 2.1 copy-start.22
  766.3 2.1 copy-start.22
  775.0 2.1 copy-start.22
  783.7 2.1 copy-start.22
  790.0 51.6 %copy-start.14 = (bf16[128,1024]{1,0:T(8,128)(2,1)S(1)}, bf16[128,1024]{1,0:T(8,128)(2,1)}, u32[]{:S(2)}) copy-start(bf16[128,1024]{1,0:T(8,128)(2,1)} %copy-done.13) | copy-start | bytes 786436
  898.3 5.9 copy-start.41
  898.3 5.9 copy-start.43
  898.3 6.0 copy-start.30
  898.3 6.2 copy-start.46
  898.3 42.0 %all-to-all-start.5 = ((bf16[32,1,20,1024]{3,2,1,0:T(8,128)(2,1)}), bf16[32,1,20,1024]{3,2,1,0:T(8,128)(2,1)}, u32[]{:S(2)}, u32[]{:S(2)}) async-start(bf16[32,1,20,1024]{3,2,1,0:T(8,128)(2,1)} %copy.99), calls=%async_computation.5 | async-start | bytes 3145728 | tf_op jit(solution)/shard_map/all_to_all | solution.py:173
  904.2 91.1 %all-reduce.17.cloned.1.call-start = ((), (), s32[]{:S(2)}) async-start(), calls=%async_computation.14 | async-start | bytes 1048576 | tf_op jit(solution)/shard_map/psum | solution.py:188
  946.9 2.3 copy-start.47
  948.3 46.9 %copy-start.20 = (f32[128,1024]{1,0:T(8,128)S(1)}, f32[128,1024]{1,0:T(8,128)}, u32[]{:S(2)}) copy-start(f32[128,1024]{1,0:T(8,128)} %all-reduce.15.cloned.1.call-done) | copy-start | bytes 1572868
  948.3 46.9 %copy-start.26 = (bf16[128,1024]{1,0:T(8,128)(2,1)S(1)}, bf16[128,1024]{1,0:T(8,128)(2,1)}, u32[]{:S(2)}) copy-start(bf16[128,1024]{1,0:T(8,128)(2,1)} %copy-done.25) | copy-start | bytes 786436
  949.2 47.2 %copy-start.27 = (bf16[1,128,1024]{2,1,0:T(8,128)(2,1)S(1)}, bf16[1,128,1024]{2,1,0:T(8,128)(2,1)}, u32[]{:S(2)}) copy-start(bf16[1,128,1024]{2,1,0:T(8,128)(2,1)} %get-tuple-element.669) | copy-start | bytes 786436
  (57 other events, 78.1 us)
Sparse Core Ops, SparseCore 0:
  14.3 85.9 all-gather.3
  138.5 48.3 all-reduce.6
  291.8 45.8 all-reduce.8
  344.0 83.6 all-gather.5
  465.9 48.3 all-reduce.10
  618.5 45.9 all-reduce.12
  671.6 83.6 all-gather.7
  793.3 48.3 all-reduce.14
  949.4 45.8 all-reduce.16
where the time goes:
time: 1010 us; the launch traced here: 1000 us
  waiting for transfers between devices  619 us (61%)
  blocking collectives  141 us (14%)
  other arithmetic  82.9 us (8%)
  local copies, waits for them, and re-layouts  77.7 us (8%)
  matrix products  45.3 us (4%)
  starting transfers between devices  20.6 us (2%)
  between operations  16.4 us (2%)
    all_gather x3, waiting for transfers between devices, per_device(): piece = lax.all_gather(keys_vals, 'tok', axis=0, tiled=True)  242 us
    all_to_all x3, blocking collectives, per_device(): lax.all_to_all(copies, 'tok', split_axis=0, concat_axis=0, tiled=True)  141 us
    psum x3, waiting for transfers between devices, per_device(): mid = resid + lax.psum(attn_part, 'rep')  139 us
    psum x3, waiting for transfers between devices, per_device(): expert_total = lax.psum(expert_local, 'rep')  133 us
    all_to_all x3, waiting for transfers between devices, per_device(): lax.all_to_all(jnp.einsum('secf,efd->secd', hidden, w_down, preferred_ele...  102 us
    slice x12, local copies, waits for them, and re-layouts, attend(): keys_vals[:, 1].reshape(rows_key, heads_here, head_size).astype(jnp.float32)  25.2 us
  transfers between devices with their start and end apart: 14, of which 14 were waited for; matrix products, arithmetic and copies ran while one was open for 3% of the time, Pallas kernels for 0%

commit v1 on v0

--- a/solution.py
+++ b/solution.py
@@ -141,7 +141,7 @@
             .astype(jnp.bfloat16)
         )
         attn_part = jnp.dot(context, w_out, preferred_element_type=jnp.float32)
-        mid = resid + lax.psum(attn_part, "rep")
+        mid = resid + jnp.sum(lax.all_gather(attn_part, "rep"), axis=0)
         normed_mid = rms_scale(mid, gains[1]).astype(jnp.bfloat16)
         logits = jnp.dot(normed_mid, w_router, preferred_element_type=jnp.float32)
         expert_ids = jnp.arange(experts_all, dtype=jnp.int32)

time: 1010 us -> 967 us (0.957)
  waiting for transfers between devices: 619 us -> 579 us
    psum x3 -> x0, waiting for transfers between devices: 139 us -> none  [per_device(): mid = resid + lax.psum(attn_part, 'rep')]
    all_gather x0 -> x3, waiting for transfers between devices: none -> 93 us  [per_device(): mid = resid + jnp.sum(lax.all_gather(attn_part, 'rep'), axis=0)]
  transfers between devices with their start and end apart: 14 -> 14, of which waited for: 14 -> 14; matrix products, arithmetic and copies ran while one was open for 3% -> 2% of each run, Pallas kernels for 0% -> 0%
where the time goes in v1:
time: 967 us; the launch traced here: 964 us
  waiting for transfers between devices  579 us (60%)
  blocking collectives  147 us (15%)
  other arithmetic  78.9 us (8%)
  local copies, waits for them, and re-layouts  75.9 us (8%)
  matrix products  45.8 us (5%)
  starting transfers between devices  20.4 us (2%)
  between operations  16.4 us (2%)
    all_gather x3, waiting for transfers between devices, per_device(): piece = lax.all_gather(keys_vals, 'tok', axis=0, tiled=True)  249 us
    all_to_all x3, blocking collectives, per_device(): lax.all_to_all(copies, 'tok', split_axis=0, concat_axis=0, tiled=True)  147 us
    psum x3, waiting for transfers between devices, per_device(): expert_total = lax.psum(expert_local, 'rep')  126 us
    all_to_all x3, waiting for transfers between devices, per_device(): lax.all_to_all(jnp.einsum('secf,efd->secd', hidden, w_down, preferred_ele...  109 us
    all_gather x3, waiting for transfers between devices, per_device(): mid = resid + jnp.sum(lax.all_gather(attn_part, 'rep'), axis=0)  93 us
    slice x12, local copies, waits for them, and re-layouts, attend(): keys_vals[:, 1].reshape(rows_key, heads_here, head_size).astype(jnp.float32)  25.2 us
  transfers between devices with their start and end apart: 14, of which 14 were waited for; matrix products, arithmetic and copies ran while one was open for 2% of the time, Pallas kernels for 0%

profile of v1, /device:TPU:8, one launch (start us, length us, event | category | flops | bytes accessed | tf_op | source)
XLA Modules:
  0.0 964.3 jit_solution(7476454365511821823)
XLA Ops:
  9.3 1.7 copy.83
  17.8 82.5 %all-gather.10.cloned.1.call-done = bf16[4096,2,256]{0,2,1:T(8,128)(2,1)} async-done(((bf16[128,2,256]{0,2,1:T(8,128)(2,1)}), bf16[4096,2,256]{0,2,1:T(8,128)(2,1)}) %all-gather.10.cloned.1.call-update) | async-done | bytes 4194320 | tf_op jit(solution)/shard_map/all_gather | solution.py:120
  100.3 34.6 %while.54 = (s32[]{:T(128)}, f32[4,128]{1,0:T(4,128)S(1)}, f32[4,128]{1,0:T(4,128)S(1)}, f32[4,128,64]{1,2,0:T(8,128)}, s32[128]{0:T(128)}, /*index=5*/s32[4096]...) while((s32[]{:T(128)}, f32[4,128]{1,0:T(4,128)S(1)}, ...), condition=%wide.region_4.5_spmd.clone, body=%wide.region_1.4_spmd.clone.sunk | while | flops 476548736 | bytes 14800775 | solution.py:134
  101.0 1.6 compare_and_fusion.9
  102.6 2.1 constant_dynamic-slice_fusion.18
  109.6 1.6 compare_and_fusion.9
  111.2 2.1 constant_dynamic-slice_fusion.18
  118.3 1.6 compare_and_fusion.9
  119.9 2.1 constant_dynamic-slice_fusion.18
  127.0 1.6 compare_and_fusion.9
  128.5 2.1 constant_dynamic-slice_fusion.18
  135.9 2.1 fusion.105
  140.4 31.3 %all-gather.16.cloned.1.call-done = f32[512,1024]{1,0:T(8,128)} async-done(((f32[128,1024]{1,0:T(8,128)}), f32[512,1024]{1,0:T(8,128)}) %all-gather.16.cloned.1.call-update) | async-done | bytes 2097168 | tf_op jit(solution)/shard_map/all_gather | solution.py:144
  171.7 1.8 reduce_sum.318
  174.4 49.1 %all_to_all.30 = bf16[32,1,20,1024]{3,2,1,0:T(8,128)(2,1)S(1)} all-to-all(bf16[32,1,20,1024]{3,2,1,0:T(8,128)(2,1)S(1)} %bitcast.396), channel_id=1, replica_groups=mesh['section'=2,'tok'=32,'rep'=4] {'tok'}, dimensions={0} | all-to-all | bytes 2621440 | tf_op jit(solution)/shard_map/all_to_all | solution.py:168
  223.5 1.8 convolution_bitcast_fusion.2
  226.3 1.9 copy.87
  228.2 5.6 all-to-all-start.1
  236.9 35.2 %all-to-all-done.1 = bf16[32,1,20,1024]{3,2,1,0:T(8,128)(2,1)S(1)} async-done(((bf16[32,1,20,1024]{3,2,1,0:T(8,128)(2,1)}), bf16[32,1,20,1024]{3,2,1,0:T(8,128)(2,1)S(1)}, u32[]{:S(2)}, u32[]{:S(2)}) %all-to-all-start.1) | async-done | bytes 1310752 | tf_op jit(solution)/shard_map/all_to_all | solution.py:173
  275.1 2.3 gather_fusion
  279.8 43.7 %all-reduce.4.cloned.1.call-done = f32[128,1024]{1,0:T(8,128)} async-done(((f32[128,1024]{1,0:T(8,128)}), f32[128,1024]{1,0:T(8,128)}) %all-reduce.4.cloned.1.call-update) | async-done | bytes 524304 | tf_op jit(solution)/shard_map/psum | solution.py:188
  331.2 83.1 %all-gather.12.cloned.1.call-done = bf16[4096,2,256]{0,2,1:T(8,128)(2,1)} async-done(((bf16[128,2,256]{0,2,1:T(8,128)(2,1)}), bf16[4096,2,256]{0,2,1:T(8,128)(2,1)}) %all-gather.12.cloned.1.call-update) | async-done | bytes 4194320 | tf_op jit(solution)/shard_map/all_gather | solution.py:120
  414.3 34.5 %while.55 = (s32[]{:T(128)}, f32[4,128]{1,0:T(4,128)S(1)}, f32[4,128]{1,0:T(4,128)S(1)}, f32[4,128,64]{1,2,0:T(8,128)}, s32[128]{0:T(128)}, /*index=5*/s32[4096]...) while((s32[]{:T(128)}, f32[4,128]{1,0:T(4,128)S(1)}, ...), condition=%wide.region_21.23_spmd.clone, body=%wide.region_18.22_spmd.clone.sunk | while | flops 476548736 | bytes 14800775 | solution.py:134
  415.0 1.6 compare_and_fusion.10
  416.6 2.1 constant_dynamic-slice_fusion.19
  423.6 1.6 compare_and_fusion.10
  425.2 2.1 constant_dynamic-slice_fusion.19
  432.3 1.6 compare_and_fusion.10
  433.8 2.1 constant_dynamic-slice_fusion.19
  440.9 1.6 compare_and_fusion.10
  442.4 2.1 constant_dynamic-slice_fusion.19
  449.8 2.1 fusion.103
  456.8 28.7 %all-gather.18.cloned.1.call-done = f32[512,1024]{1,0:T(8,128)} async-done(((f32[128,1024]{1,0:T(8,128)}), f32[512,1024]{1,0:T(8,128)}) %all-gather.18.cloned.1.call-update) | async-done | bytes 2097168 | tf_op jit(solution)/shard_map/all_gather | solution.py:144
  485.6 1.8 reduce_sum.329
  489.0 49.1 %all_to_all.31 = bf16[32,1,20,1024]{3,2,1,0:T(8,128)(2,1)S(1)} all-to-all(bf16[32,1,20,1024]{3,2,1,0:T(8,128)(2,1)S(1)} %bitcast.397), channel_id=1, replica_groups=mesh['section'=2,'tok'=32,'rep'=4] {'tok'}, dimensions={0} | all-to-all | bytes 2621440 | tf_op jit(solution)/shard_map/all_to_all | solution.py:168
  538.1 1.8 convolution_bitcast_fusion.1
  540.9 2.0 copy.93
  542.8 5.7 all-to-all-start.3
  551.5 35.4 %all-to-all-done.3 = bf16[32,1,20,1024]{3,2,1,0:T(8,128)(2,1)S(1)} async-done(((bf16[32,1,20,1024]{3,2,1,0:T(8,128)(2,1)}), bf16[32,1,20,1024]{3,2,1,0:T(8,128)(2,1)S(1)}, u32[]{:S(2)}, u32[]{:S(2)}) %all-to-all-start.3) | async-done | bytes 1310752 | tf_op jit(solution)/shard_map/all_to_all | solution.py:173
  586.9 1.6 convert_reduce_fusion.1
  589.9 2.3 gather_fusion.1
  594.6 43.7 %all-reduce.6.cloned.1.call-done = f32[128,1024]{1,0:T(8,128)} async-done(((f32[128,1024]{1,0:T(8,128)}), f32[128,1024]{1,0:T(8,128)}) %all-reduce.6.cloned.1.call-update) | async-done | bytes 524304 | tf_op jit(solution)/shard_map/psum | solution.py:188
  638.3 2.1 select_bitcast_fusion
  646.2 82.9 %all-gather.14.cloned.1.call-done = bf16[4096,2,256]{0,2,1:T(8,128)(2,1)} async-done(((bf16[128,2,256]{0,2,1:T(8,128)(2,1)}), bf16[4096,2,256]{0,2,1:T(8,128)(2,1)}) %all-gather.14.cloned.1.call-update) | async-done | bytes 4194320 | tf_op jit(solution)/shard_map/all_gather | solution.py:120
  729.1 34.7 %while.56 = (s32[]{:T(128)}, f32[4,128]{1,0:T(4,128)S(1)}, f32[4,128]{1,0:T(4,128)S(1)}, f32[4,128,64]{1,2,0:T(8,128)}, s32[128]{0:T(128)}, /*index=5*/s32[4096]...) while((s32[]{:T(128)}, f32[4,128]{1,0:T(4,128)S(1)}, ...), condition=%wide.region_38.40_spmd.clone, body=%wide.region_35.39_spmd.clone.sunk | while | flops 476548736 | bytes 14800775 | solution.py:134
  729.8 1.6 compare_and_fusion.11
  731.3 2.1 constant_dynamic-slice_fusion.20
  738.4 1.6 compare_and_fusion.11
  740.0 2.1 constant_dynamic-slice_fusion.20
  747.1 1.6 compare_and_fusion.11
  748.7 2.1 constant_dynamic-slice_fusion.20
  755.7 1.6 compare_and_fusion.11
  757.3 2.1 constant_dynamic-slice_fusion.20
  764.7 2.1 fusion.101
  767.5 32.9 %all-gather.20.cloned.1.call-done = f32[512,1024]{1,0:T(8,128)} async-done(((f32[128,1024]{1,0:T(8,128)}), f32[512,1024]{1,0:T(8,128)}) %all-gather.20.cloned.1.call-update) | async-done | bytes 2097168 | tf_op jit(solution)/shard_map/all_gather | solution.py:144
  800.5 1.8 reduce_sum.339
  805.2 49.1 %all_to_all.32 = bf16[32,1,20,1024]{3,2,1,0:T(8,128)(2,1)S(1)} all-to-all(bf16[32,1,20,1024]{3,2,1,0:T(8,128)(2,1)S(1)} %bitcast.398), channel_id=1, replica_groups=mesh['section'=2,'tok'=32,'rep'=4] {'tok'}, dimensions={0} | all-to-all | bytes 2621440 | tf_op jit(solution)/shard_map/all_to_all | solution.py:168
  854.3 1.8 convolution_bitcast_fusion
  857.0 1.9 copy.99
  858.9 5.8 all-to-all-start.5
  865.0 38.0 %all-to-all-done.5 = bf16[32,1,20,1024]{3,2,1,0:T(8,128)(2,1)} async-done(((bf16[32,1,20,1024]{3,2,1,0:T(8,128)(2,1)}), bf16[32,1,20,1024]{3,2,1,0:T(8,128)(2,1)}, u32[]{:S(2)}, u32[]{:S(2)}) %all-to-all-start.5) | async-done | bytes 1310752 | tf_op jit(solution)/shard_map/all_to_all | solution.py:173
  903.0 3.1 convert_reduce_fusion
  907.6 2.1 gather_fusion.2
  916.8 39.0 %all-reduce.8.cloned.1.call-done = f32[128,1024]{1,0:T(8,128)} async-done(((f32[128,1024]{1,0:T(8,128)}), f32[128,1024]{1,0:T(8,128)}) %all-reduce.8.cloned.1.call-update) | async-done | bytes 524304 | tf_op jit(solution)/shard_map/psum | solution.py:188
  (451 shorter events, 124.1 us)
Async XLA Ops:
  7.2 216.4 %copy-start = (bf16[1,1,1024,2,352]{2,4,3,1,0:T(8,128)(2,1)S(1)}, bf16[1,1,1024,2,352]{2,4,3,1,0:T(8,128)(2,1)}, u32[]{:S(2)}) copy-start(bf16[1,1,1024,2,352]{2,4,3,1,0:T(8,128)(2,1)} %param.26) | copy-start | bytes 4325380
  7.2 3.9 copy-start.17
  7.2 93.1 %all-gather.10.cloned.1.call-start = ((), (), s32[]{:S(2)}) async-start(), calls=%async_computation.6 | async-start | bytes 4325376 | tf_op jit(solution)/shard_map/all_gather | solution.py:120
  9.3 3.1 copy-start.35
  11.0 89.3 %copy-start.7 = (bf16[1,1024,3,256]{1,3,2,0:T(8,128)(2,1)}, bf16[1,1024,3,256]{1,3,2,0:T(8,128)(2,1)S(1)}, u32[]{:S(2)}) copy-start(bf16[1,1024,3,256]{1,3,2,0:T(8,128)(2,1)S(1)} %copy.83) | copy-start | bytes 4718596
  14.2 157.5 %all-gather.16.cloned.1.call-start = ((), (), s32[]{:S(2)}) async-start(), calls=%async_computation.12 | async-start | bytes 2621440 | tf_op jit(solution)/shard_map/all_gather | solution.py:144
  102.6 2.1 copy-start.1
  102.6 2.1 copy-start.20
  111.2 2.1 copy-start.1
  111.2 2.1 copy-start.20
  119.9 2.1 copy-start.1
  119.9 2.1 copy-start.20
  128.5 2.1 copy-start.1
  128.5 2.1 copy-start.20
  135.9 37.6 %copy-start.18 = (bf16[2,128,1024]{2,1,0:T(8,128)(2,1)S(1)}, bf16[2,128,1024]{2,1,0:T(8,128)(2,1)}, u32[]{:S(2)}) copy-start(bf16[2,128,1024]{2,1,0:T(8,128)(2,1)} %param.18) | copy-start | bytes 1572868
  223.5 1.8 copy-start.46
  228.2 43.9 %all-to-all-start.1 = ((bf16[32,1,20,1024]{3,2,1,0:T(8,128)(2,1)}), bf16[32,1,20,1024]{3,2,1,0:T(8,128)(2,1)S(1)}, u32[]{:S(2)}, u32[]{:S(2)}) async-start(bf16[32,1,20,1024]{3,2,1,0:T(8,128)(2,1)} %copy.87), calls=%async_computation.1 | async-start | bytes 3145728 | tf_op jit(solution)/shard_map/all_to_all | solution.py:173
  233.7 89.8 %all-reduce.4.cloned.1.call-start = ((), (), s32[]{:S(2)}) async-start(), calls=%async_computation.7 | async-start | bytes 1048576 | tf_op jit(solution)/shard_map/psum | solution.py:188
  275.1 2.3 copy-start.43
  278.8 50.2 %copy-start.8 = (bf16[1,1024,3,256]{1,3,2,0:T(8,128)(2,1)S(1)}, bf16[1,1024,3,256]{1,3,2,0:T(8,128)(2,1)}, u32[]{:S(2)}) copy-start(bf16[1,1024,3,256]{1,3,2,0:T(8,128)(2,1)} %copy-done.7) | copy-start | bytes 4718596
  278.8 50.2 %copy-start.36 = (f32[1,1,1024]{2,1,0:T(1,128)S(1)}, f32[1,1,1024]{2,1,0:T(1,128)}, u32[]{:S(2)}) copy-start(f32[1,1,1024]{2,1,0:T(1,128)} %copy-done.35) | copy-start | bytes 12292
  279.7 134.6 %all-gather.12.cloned.1.call-start = ((), (), s32[]{:S(2)}) async-start(), calls=%async_computation.8 | async-start | bytes 4325376 | tf_op jit(solution)/shard_map/all_gather | solution.py:120
  324.7 2.4 collective-permute-start
  330.5 155.0 %all-gather.18.cloned.1.call-start = ((), (), s32[]{:S(2)}) async-start(), calls=%async_computation.13 | async-start | bytes 2621440 | tf_op jit(solution)/shard_map/all_gather | solution.py:144
  416.6 2.1 copy-start.3
  416.6 2.1 copy-start.22
  425.2 2.1 copy-start.3
  425.2 2.1 copy-start.22
  433.8 2.1 copy-start.3
  433.8 2.1 copy-start.22
  442.4 2.1 copy-start.3
  442.4 2.1 copy-start.22
  449.8 37.6 %copy-start.16 = (bf16[128,1024]{1,0:T(8,128)(2,1)S(1)}, bf16[128,1024]{1,0:T(8,128)(2,1)}, u32[]{:S(2)}) copy-start(bf16[128,1024]{1,0:T(8,128)(2,1)} %copy-done.15) | copy-start | bytes 786436
  538.1 1.8 copy-start.47
  542.8 5.8 copy-start.39
  542.8 44.0 %all-to-all-start.3 = ((bf16[32,1,20,1024]{3,2,1,0:T(8,128)(2,1)}), bf16[32,1,20,1024]{3,2,1,0:T(8,128)(2,1)S(1)}, u32[]{:S(2)}, u32[]{:S(2)}) async-start(bf16[32,1,20,1024]{3,2,1,0:T(8,128)(2,1)} %copy.93), calls=%async_computation.3 | async-start | bytes 3145728 | tf_op jit(solution)/shard_map/all_to_all | solution.py:173
  548.5 89.8 %all-reduce.6.cloned.1.call-start = ((), (), s32[]{:S(2)}) async-start(), calls=%async_computation.9 | async-start | bytes 1048576 | tf_op jit(solution)/shard_map/psum | solution.py:188
  589.9 2.3 copy-start.44
  594.5 49.2 %copy-start.9 = (bf16[1,1024,3,256]{1,3,2,0:T(8,128)(2,1)S(1)}, bf16[1,1024,3,256]{1,3,2,0:T(8,128)(2,1)}, u32[]{:S(2)}) copy-start(bf16[1,1024,3,256]{1,3,2,0:T(8,128)(2,1)} %copy-done.7) | copy-start | bytes 4718596
  594.5 49.2 %copy-start.37 = (f32[1,1,1024]{2,1,0:T(1,128)S(1)}, f32[1,1,1024]{2,1,0:T(1,128)}, u32[]{:S(2)}) copy-start(f32[1,1,1024]{2,1,0:T(1,128)} %copy-done.35) | copy-start | bytes 12292
  594.5 134.6 %all-gather.14.cloned.1.call-start = ((), (), s32[]{:S(2)}) async-start(), calls=%async_computation.10 | async-start | bytes 4325376 | tf_op jit(solution)/shard_map/all_gather | solution.py:120
  638.3 4.5 copy-start.19
  640.4 2.6 copy-start.24
  640.4 2.4 collective-permute-start.1
  645.3 155.2 %all-gather.20.cloned.1.call-start = ((), (), s32[]{:S(2)}) async-start(), calls=%async_computation.14 | async-start | bytes 2621440 | tf_op jit(solution)/shard_map/all_gather | solution.py:144
  731.3 2.1 copy-start.5
  731.3 2.1 copy-start.21
  740.0 2.1 copy-start.5
  740.0 2.1 copy-start.21
  748.7 2.1 copy-start.5
  748.7 2.1 copy-start.21
  757.3 2.1 copy-start.5
  757.3 2.1 copy-start.21
  764.6 37.6 %copy-start.14 = (bf16[128,1024]{1,0:T(8,128)(2,1)S(1)}, bf16[128,1024]{1,0:T(8,128)(2,1)}, u32[]{:S(2)}) copy-start(bf16[128,1024]{1,0:T(8,128)(2,1)} %copy-done.13) | copy-start | bytes 786436
  854.3 1.8 copy-start.48
  858.9 5.8 copy-start.38
  858.9 5.8 copy-start.40
  858.9 5.9 copy-start.28
  858.9 6.0 copy-start.41
  858.9 44.2 %all-to-all-start.5 = ((bf16[32,1,20,1024]{3,2,1,0:T(8,128)(2,1)}), bf16[32,1,20,1024]{3,2,1,0:T(8,128)(2,1)}, u32[]{:S(2)}, u32[]{:S(2)}) async-start(bf16[32,1,20,1024]{3,2,1,0:T(8,128)(2,1)} %copy.99), calls=%async_computation.5 | async-start | bytes 3145728 | tf_op jit(solution)/shard_map/all_to_all | solution.py:173
  864.6 91.1 %all-reduce.8.cloned.1.call-start = ((), (), s32[]{:S(2)}) async-start(), calls=%async_computation.11 | async-start | bytes 1048576 | tf_op jit(solution)/shard_map/psum | solution.py:188
  909.7 2.3 copy-start.42
  911.0 44.7 %copy-start.25 = (bf16[128,1024]{1,0:T(8,128)(2,1)S(1)}, bf16[128,1024]{1,0:T(8,128)(2,1)}, u32[]{:S(2)}) copy-start(bf16[128,1024]{1,0:T(8,128)(2,1)} %copy-done.24) | copy-start | bytes 786436
  912.0 45.0 %copy-start.26 = (bf16[1,128,1024]{2,1,0:T(8,128)(2,1)S(1)}, bf16[1,128,1024]{2,1,0:T(8,128)(2,1)}, u32[]{:S(2)}) copy-start(bf16[1,128,1024]{2,1,0:T(8,128)(2,1)} %get-tuple-element.669) | copy-start | bytes 786436
  (53 other events, 68.6 us)
Sparse Core Ops, SparseCore 0:
  14.3 85.9 all-gather.9
  138.2 33.4 all-gather.15
  279.8 43.6 all-reduce.3
  330.6 83.6 all-gather.11
  452.0 33.4 all-gather.17
  594.6 43.6 all-reduce.5
  645.4 83.6 all-gather.13
  766.9 33.4 all-gather.19
  912.1 43.6 all-reduce.7
